TPU v7x, 128 devices: a whole 4x4x4 slice. The times are simulated.
128 devices in a mesh: layer: 16 (over y, x), prow: 4 (over z), pcol: 2 (over core).
Axes of the slice: x: 4, y: 4, z: 4, core: 2. Of those that a mesh axis runs over, the one named last changes fastest.
Arguments:
- front: bfloat16 [16, 2048, 32768], P('layer', 'prow', 'pcol'), may hold values from -6 to 6
- pivots: bfloat16 [16, 2, 256, 32768], P('layer', None, 'prow', 'pcol'), may hold values from -0.8984375 to 0.8984375
- inverses: bfloat16 [16, 2, 256, 256], P('layer'), may hold values from -0.1875 to 0.1875
- slab_pattern: int32 [16, 8, 128], P('layer', 'prow', 'pcol'), may hold values 0 or 1
- pivot_pattern: int32 [16, 2, 128], P('layer', None, 'pcol'), may hold values from 0 to 1, as said below
Outputs:
- ancestor: float32 [4, 16, 32, 32768], P('prow', 'layer', None, 'pcol')
- lower: bfloat16 [16, 2048, 512], P('layer', 'prow')
- upper: bfloat16 [16, 256, 32768], P('layer', 'prow', 'pcol')
Inputs may be any that keep to these rules, and one draw needn't show every extreme that they name: `pivot_pattern`: each entry says whether that block of the pivot rows is structurally nonzero. `slab_pattern`: each entry says whether that block of the front rows is structurally nonzero.
All inputs are finite; a program needn't handle non-finite values.
Results may differ from a plain program's by a relative error of at most 0.014.
Values may be sent and summed in bfloat16 or wider, within the bound.
No kernel may reach another device: no remote copies, remote signals or barrier semaphores. Data moves between devices by JAX's collectives and lax.ppermute only.
A program may use at most 192 MiB of HBM per device.

v0:
```python
import jax
import jax.numpy as jnp
from jax import lax
from jax.sharding import PartitionSpec as P


def spread(value, axis, root):
    mine = lax.axis_index(axis) == root
    return lax.psum(jnp.where(mine, value, jnp.zeros_like(value)), axis)


def on_device(front, pivots, inverses, slab_pattern, pivot_pattern):
    block_size = inverses.shape[-1]
    panel_width = 2 * block_size
    row_count = front.shape[1]
    col_count = front.shape[2]
    own_rows = pivots.shape[2]
    masked = (
        front[0].reshape(row_count // block_size, block_size, col_count // block_size, block_size)
        * slab_pattern[0].astype(jnp.bfloat16)[:, None, :, None]
    ).reshape(row_count, col_count)
    pivot_masked = (
        pivots[0].reshape(2, own_rows, col_count // block_size, block_size)
        * pivot_pattern[0].astype(jnp.bfloat16)[:, None, :, None]
    ).reshape(2, own_rows, col_count)
    first_inverse = inverses[0, 0]
    second_inverse = inverses[0, 1]
    row_offset = lax.axis_index("prow") * own_rows
    gathered = lax.all_gather(pivot_masked, "prow", axis=1, tiled=True)
    panel_cols = spread(
        jnp.concatenate(
            [masked[:, :panel_width], gathered[0][:, :panel_width], gathered[1][:, :panel_width]], 0
        ),
        "pcol",
        0,
    )
    front_cols = panel_cols[:row_count]
    pivot_cols = panel_cols[row_count : row_count + block_size]
    second_cols = panel_cols[row_count + block_size :]
    lower_pivot = jnp.dot(
        second_cols[:, :block_size], first_inverse, preferred_element_type=jnp.float32
    ).astype(jnp.bfloat16)
    upper_first = gathered[0]
    upper_second = (
        gathered[1].astype(jnp.float32)
        - jnp.dot(lower_pivot, upper_first, preferred_element_type=jnp.float32)
    ).astype(jnp.bfloat16)
    upper_own = lax.dynamic_slice_in_dim(upper_second, row_offset, own_rows, 0)
    lower_first = jnp.dot(
        front_cols[:, :block_size], first_inverse, preferred_element_type=jnp.float32
    ).astype(jnp.bfloat16)
    carried = (
        front_cols[:, block_size:].astype(jnp.float32)
        - jnp.dot(
            lower_first, pivot_cols[:, block_size:panel_width], preferred_element_type=jnp.float32
        )
    ).astype(jnp.bfloat16)
    lower_second = jnp.dot(carried, second_inverse, preferred_element_type=jnp.float32).astype(
        jnp.bfloat16
    )
    lower_panel = jnp.concatenate([lower_first, lower_second], 1)
    stacked = jnp.concatenate([upper_first, upper_second], 0)
    col_index = lax.axis_index("pcol") * col_count + jnp.arange(col_count, dtype=jnp.int32)
    retained = col_index >= panel_width
    schur_rows = masked.astype(jnp.float32) - jnp.dot(
        lower_panel, stacked, preferred_element_type=jnp.float32
    )
    schur_rows = jnp.where(retained[None, :], schur_rows, jnp.zeros_like(schur_rows))
    summed = lax.psum_scatter(
        schur_rows.astype(jnp.bfloat16), "layer", scatter_dimension=0, tiled=True
    ).astype(jnp.float32)
    ancestor = summed.reshape(1, 1, summed.shape[0], col_count)
    return (ancestor, lower_panel[None], upper_own[None])


def solution(mesh):
    placed = (
        P("layer", "prow", "pcol"),
        P("layer", None, "prow", "pcol"),
        P("layer", None, None, None),
        P("layer", "prow", "pcol"),
        P("layer", None, "pcol"),
    )
    return jax.shard_map(
        on_device,
        mesh=mesh,
        in_specs=placed,
        out_specs=(
            P("prow", "layer", None, "pcol"),
            P("layer", "prow", None),
            P("layer", "prow", "pcol"),
        ),
        check_vma=False,
    )
```

profile of v0, /device:TPU:0, one launch (start us, length us, event | category | flops | bytes accessed | tf_op | source)
XLA Modules:
  0.0 362.3 jit_solution(13036660158709411677)
XLA Ops:
  7.2 0.0 all-gather.2.cloned.1.call-start
  7.2 0.7 convert_bitcast_fusion
  7.9 0.1 broadcast_bitcast_fusion
  8.0 0.1 copy.10
  8.1 4.8 %bitcast_multiply_fusion.1 = bf16[2,64,16384]{2,1,0:T(8,128)(2,1)} fusion(bf16[1,2,64,16384]{3,2,1,0:T(8,128)(2,1)} %param.6, bf16[2,16384]{1,0:T(2,128)(2,1)S(1)} %bitcast.40), kind=kLoop, calls=%fused_computation.9 | loop fusion | flops 2097152 | bytes 8454144 | tf_op jit(solution)/shard_map/mul | solution.py:23
  12.8 0.0 all-gather.2.cloned.1.call-update
  12.9 0.0 all-reduce.2.cloned.1.call-start
  12.9 0.7 convert_bitcast_fusion.1
  13.6 2.7 mul.31
  16.3 10.4 %copy.9 = bf16[64,8,64,256]{3,1,2,0:T(8,128)(2,1)S(1)} copy(bf16[64,8,64,256]{3,2,1,0:T(8,128)(2,1)S(1)} %bitcast.39) | data formatting | bytes 33554432
  26.8 9.8 %bitcast_multiply_fusion = bf16[512,16384]{1,0:T(8,128)(2,1)S(1)} fusion(bf16[512,16384]{1,0:T(8,128)(2,1)S(1)} %bitcast.38, bf16[1,512,16384]{2,1,0:T(8,128)(2,1)} %param.5), kind=kLoop, calls=%fused_computation.6 | loop fusion | flops 8388608 | bytes 50331648 | tf_op jit(solution)/shard_map/mul | solution.py:19
  36.6 0.0 copy-start
  36.6 5.7 %copy-done = bf16[512,16384]{1,0:T(8,128)(2,1)} copy-done((bf16[512,16384]{1,0:T(8,128)(2,1)}, bf16[512,16384]{1,0:T(8,128)(2,1)S(1)}, u32[]{:S(2)}) %copy-start) | copy-done | bytes 16777240
  42.3 0.0 copy-start.2
  42.3 127.3 %all-gather.2.cloned.1.call-done = bf16[2,256,16384]{2,1,0:T(8,128)(2,1)} async-done(((bf16[2,64,16384]{2,1,0:T(8,128)(2,1)}), bf16[2,256,16384]{2,1,0:T(8,128)(2,1)}) %all-gather.2.cloned.1.call-update) | async-done | bytes 16777232 | tf_op jit(solution)/shard_map/all_gather | solution.py:29
  169.7 6.7 %slice_bitcast_fusion.1 = (bf16[256,16384]{1,0:T(8,128)(2,1)S(1)}, bf16[256,16384]{1,0:T(8,128)(2,1)S(1)}) fusion(bf16[2,256,16384]{2,1,0:T(8,128)(2,1)} %all-gather.2.cloned.1.call-done), kind=kLoop, calls=%fused_computation.8 | loop fusion | bytes 33554432 | tf_op jit(solution)/shard_map/squeeze | solution.py:32
  176.4 0.0 copy-start.1
  176.4 3.2 copy-done.1
  179.6 1.2 maximum_select_fusion
  180.8 0.0 all-reduce.2.cloned.1.call-update
  180.8 0.0 reduce-scatter.2.cloned.1.call-start
  180.9 26.2 %all-reduce.2.cloned.1.call-done = bf16[1024,512]{1,0:T(8,128)(2,1)} async-done(((bf16[1024,512]{1,0:T(8,128)(2,1)}), bf16[1024,512]{1,0:T(8,128)(2,1)}) %all-reduce.2.cloned.1.call-update) | async-done | bytes 1048592 | tf_op jit(solution)/shard_map/psum | solution.py:9
  207.1 0.0 copy-done.2
  207.1 9.2 %fusion = bf16[256,16384]{1,0:T(8,128)(2,1)} fusion(bf16[1024,512]{1,0:T(8,128)(2,1)} %all-reduce.2.cloned.1.call-done, bf16[1,2,256,256]{3,2,1,0:T(8,128)(2,1)S(1)} %copy-done.2, bf16[2,256,16384]{2,1,0:T(8,128)(2,1)} %all-gather.2.cloned.1.call-done), kind=kOutput, calls=%fused_computation.2 | convolution fusion | flops 2193686528 | bytes 25427968 | tf_op jit(solution)/shard_map/dot_general | solution.py:46
  216.4 1.2 convolution_convert_fusion.1
  217.6 1.5 convolution_convert_fusion
  219.1 22.0 %select_convert_fusion = bf16[512,16384]{1,0:T(8,128)(2,1)} fusion(bf16[512,16384]{1,0:T(8,128)(2,1)} %copy-done, bf16[256,16384]{1,0:T(8,128)(2,1)} %fusion, bf16[256,16384]{1,0:T(8,128)(2,1)} %copy-done.1, pred[16384]{0:T(1024)(128)(4,1)S(1)} %add_compare_fusion, bf16[512,256]{0,1:T(8,128)(2,1)S(1)} %convolution_convert_fusion, ...), kind=kOutput, calls=%fused_computation | convolution fusion | flops 8658092032 | bytes 50872320 | tf_op jit(solution)/shard_map/dot_general | solution.py:65
  241.0 0.0 reduce-scatter.2.cloned.1.call-update
  241.1 1.0 copy.8
  242.1 3.0 dynamic-slice_bitcast_fusion
  245.2 108.0 %reduce-scatter.2.cloned.1.call-done = bf16[32,16384]{1,0:T(8,128)(2,1)} async-done(((bf16[512,16384]{1,0:T(8,128)(2,1)}), bf16[32,16384]{1,0:T(8,128)(2,1)}) %reduce-scatter.2.cloned.1.call-update) | async-done | bytes 1048592 | tf_op jit(solution)/shard_map/reduce_scatter | solution.py:69
  353.1 2.7 bitcast_convert_fusion
  (5 shorter events, 0.1 us)
Async XLA Ops:
  7.2 162.5 %all-gather.2.cloned.1.call-start = ((), (), s32[]{:S(2)}) async-start(), calls=%async_computation.1 | async-start | bytes 20971520 | tf_op jit(solution)/shard_map/all_gather | solution.py:29
  12.9 194.2 %all-reduce.2.cloned.1.call-start = ((), (), s32[]{:S(2)}) async-start(), calls=%async_computation.2 | async-start | bytes 2097152 | tf_op jit(solution)/shard_map/psum | solution.py:9
  36.6 5.7 %copy-start = (bf16[512,16384]{1,0:T(8,128)(2,1)}, bf16[512,16384]{1,0:T(8,128)(2,1)S(1)}, u32[]{:S(2)}) copy-start(bf16[512,16384]{1,0:T(8,128)(2,1)S(1)} %bitcast_multiply_fusion) | copy-start | bytes 50331652
  42.3 164.8 %copy-start.2 = (bf16[1,2,256,256]{3,2,1,0:T(8,128)(2,1)S(1)}, bf16[1,2,256,256]{3,2,1,0:T(8,128)(2,1)}, u32[]{:S(2)}) copy-start(bf16[1,2,256,256]{3,2,1,0:T(8,128)(2,1)} %param.7) | copy-start | bytes 786436
  176.4 3.2 copy-start.1
  180.8 172.3 %reduce-scatter.2.cloned.1.call-start = ((), (), s32[]{:S(2)}) async-start(), calls=%async_computation.3 | async-start | bytes 17825792 | tf_op jit(solution)/shard_map/reduce_scatter | solution.py:69
Sparse Core Ops, SparseCore 0:
  13.0 156.6 all-gather.1
  181.0 26.1 all-reduce.1
  241.2 111.8 reduce-scatter.1
where the time goes:
time: 363 us; the launch traced here: 362 us
  waiting for transfers between devices  262 us (72%)
  matrix products  33.9 us (9%)
  local copies, waits for them, and re-layouts  33.1 us (9%)
  other arithmetic  19.8 us (5%)
  between operations  13.9 us (4%)
    all_gather x1, waiting for transfers between devices, on_device(): gathered = lax.all_gather(pivot_masked, 'prow', axis=1, tiled=True)  127 us
    reduce_scatter x1, waiting for transfers between devices, on_device(): lax.psum_scatter(schur_rows.astype(jnp.bfloat16), 'layer', scatter_dimens...  108 us
    psum x1, waiting for transfers between devices, spread(): return lax.psum(jnp.where(mine, value, jnp.zeros_like(value)), axis)  26.2 us
    dot_general x1, matrix products, on_device(): jnp.dot(lower_panel, stacked, preferred_element_type=jnp.float32)  22 us
    unnamed x10, local copies, waits for them, and re-layouts  20.5 us
    mul x1, other arithmetic, on_device(): front[0]  9.77 us
    dot_general x1, matrix products, on_device(): jnp.dot(lower_pivot, upper_first, preferred_element_type=jnp.float32)  9.24 us
  transfers between devices with their start and end apart: 3, of which 3 were waited for; matrix products, arithmetic and copies ran while one was open for 8% of the time, Pallas kernels for 0%

commit v1 on v0

v1 whole, which is shorter than its diff:
```python
import jax
import jax.numpy as jnp
from jax import lax
from jax.sharding import PartitionSpec as P

CHUNKS = 4


def ring(value, axis, size, step):
    return lax.ppermute(value, axis, [(i, (i + step) % size) for i in range(size)])


def gather_relative(value, axis, size):
    from_prev = ring(value, axis, size, 1)
    from_next = ring(value, axis, size, -1)
    half = value.shape[1] // 2
    far_lo = ring(from_prev[:, :half], axis, size, 1)
    far_hi = ring(from_next[:, half:], axis, size, -1)
    far = jnp.concatenate([far_lo, far_hi], 1)
    return jnp.concatenate([value, from_next, far, from_prev], 1)


def on_device(front, pivots, inverses, slab_pattern, pivot_pattern):
    block_size = inverses.shape[-1]
    panel_width = 2 * block_size
    row_count = front.shape[1]
    col_count = front.shape[2]
    own_rows = pivots.shape[2]
    n_prow = lax.axis_size("prow")
    n_pcol = lax.axis_size("pcol")
    assert n_prow == 4
    masked = (
        front[0].reshape(row_count // block_size, block_size, col_count // block_size, block_size)
        * slab_pattern[0].astype(jnp.bfloat16)[:, None, :, None]
    ).reshape(row_count, col_count)
    pivot_masked = (
        pivots[0].reshape(2, own_rows, col_count // block_size, block_size)
        * pivot_pattern[0].astype(jnp.bfloat16)[:, None, :, None]
    ).reshape(2, own_rows, col_count)
    first_inverse = inverses[0, 0]
    second_inverse = inverses[0, 1]
    prow = lax.axis_index("prow")
    pcol = lax.axis_index("pcol")

    panel = lax.all_gather(pivot_masked[:, :, :panel_width], "prow", axis=1, tiled=True)
    lower_pivot = jnp.dot(
        panel[1][:, :block_size], first_inverse, preferred_element_type=jnp.float32
    ).astype(jnp.bfloat16)
    lower_first = jnp.dot(
        masked[:, :block_size], first_inverse, preferred_element_type=jnp.float32
    ).astype(jnp.bfloat16)
    carried = (
        masked[:, block_size:panel_width].astype(jnp.float32)
        - jnp.dot(
            lower_first, panel[0][:, block_size:panel_width], preferred_element_type=jnp.float32
        )
    ).astype(jnp.bfloat16)
    lower_second = jnp.dot(carried, second_inverse, preferred_element_type=jnp.float32).astype(
        jnp.bfloat16
    )
    lower_panel = jnp.concatenate([lower_first, lower_second], 1)
    sent = lax.ppermute((lower_panel, lower_pivot), "pcol", [(0, i) for i in range(1, n_pcol)])
    on_root = pcol == 0
    lower_panel = jnp.where(on_root, lower_panel, sent[0])
    lower_pivot = jnp.where(on_root, lower_pivot, sent[1])

    shift = prow * own_rows
    lower_rel = jnp.concatenate(
        [
            jnp.roll(lower_panel[:, :block_size], -shift, axis=1),
            jnp.roll(lower_panel[:, block_size:], -shift, axis=1),
        ],
        1,
    )
    pivot_rel = jnp.roll(jnp.roll(lower_pivot, -shift, axis=0), -shift, axis=1)

    width = col_count // CHUNKS
    summed_parts = []
    upper_parts = []
    for k in range(CHUNKS):
        cols = slice(k * width, (k + 1) * width)
        rows_rel = gather_relative(pivot_masked[:, :, cols], "prow", n_prow)
        first_rel = rows_rel[0]
        upper_rel = (
            rows_rel[1].astype(jnp.float32)
            - jnp.dot(pivot_rel, first_rel, preferred_element_type=jnp.float32)
        ).astype(jnp.bfloat16)
        upper_parts.append(upper_rel[:own_rows])
        stacked = jnp.concatenate([first_rel, upper_rel], 0)
        col_index = pcol * col_count + k * width + jnp.arange(width, dtype=jnp.int32)
        retained = col_index >= panel_width
        schur = masked[:, cols].astype(jnp.float32) - jnp.dot(
            lower_rel, stacked, preferred_element_type=jnp.float32
        )
        schur = jnp.where(retained[None, :], schur, jnp.zeros_like(schur))
        summed_parts.append(
            lax.psum_scatter(schur.astype(jnp.bfloat16), "layer", scatter_dimension=0, tiled=True)
        )
    summed = jnp.concatenate(summed_parts, 1).astype(jnp.float32)
    ancestor = summed.reshape(1, 1, summed.shape[0], col_count)
    upper_own = jnp.concatenate(upper_parts, 1)
    return (ancestor, lower_panel[None], upper_own[None])


def solution(mesh):
    placed = (
        P("layer", "prow", "pcol"),
        P("layer", None, "prow", "pcol"),
        P("layer", None, None, None),
        P("layer", "prow", "pcol"),
        P("layer", None, "pcol"),
    )
    return jax.shard_map(
        on_device,
        mesh=mesh,
        in_specs=placed,
        out_specs=(
            P("prow", "layer", None, "pcol"),
            P("layer", "prow", None),
            P("layer", "prow", "pcol"),
        ),
        check_vma=False,
    )
```

time: 363 us -> 441 us (1.21)
  blocking collectives: 0 us -> 32.2 us
  starting transfers between devices: 0.12 us -> 31.1 us
  local copies, waits for them, and re-layouts: 33.1 us -> 45.3 us
    all_gather x1 -> x0, waiting for transfers between devices: 127 us -> none  [on_device(): gathered = lax.all_gather(pivot_masked, 'prow', axis=1, tiled=True)]
    ppermute x0 -> x18, waiting for transfers between devices: none -> 102 us  [the longest x16 101 us: ring(): lax.ppermute(value, axis, [(i, (i + step) % size) for i in range(size)])]
    reduce_scatter x1 -> x4, waiting for transfers between devices: 108 us -> 163 us  [on_device(): lax.psum_scatter(schur.astype(jnp.bfloat16), 'layer', scatter_dimension=0...]
    all_gather x0 -> x1, blocking collectives: none -> 32.2 us  [on_device(): lax.all_gather(pivot_masked[:, :, :panel_width], 'prow', axis=1, tiled=True)]
    ppermute x0 -> x18, starting transfers between devices: none -> 31 us  [the longest x16 27.6 us: ring(): lax.ppermute(value, axis, [(i, (i + step) % size) for i in range(size)])]
    psum x1 -> x0, waiting for transfers between devices: 26.2 us -> none  [spread(): return lax.psum(jnp.where(mine, value, jnp.zeros_like(value)), axis)]
    unnamed x10 -> x40, local copies, waits for them, and re-layouts: 20.5 us -> 33.3 us
    squeeze x1 -> x5, local copies, waits for them, and re-layouts: 6.73 us -> 0.58 us  [the longest x4 0.54 us: on_device(): first_rel = rows_rel[0]]
  transfers between devices with their start and end apart: 3 -> 22, of which waited for: 3 -> 12; matrix products, arithmetic and copies ran while one was open for 8% -> 15% of each run, Pallas kernels for 0% -> 0%
where the time goes in v1:
time: 441 us
  waiting for transfers between devices  265 us (60%)
  local copies, waits for them, and re-layouts  45.3 us (10%)
  matrix products  34.9 us (8%)
  blocking collectives  32.2 us (7%)
  starting transfers between devices  31.1 us (7%)
  other arithmetic  17.7 us (4%)
  between operations  14.2 us (3%)
    reduce_scatter x4, waiting for transfers between devices, on_device(): lax.psum_scatter(schur.astype(jnp.bfloat16), 'layer', scatter_dimension=0...  163 us
    ppermute x16, waiting for transfers between devices, ring(): lax.ppermute(value, axis, [(i, (i + step) % size) for i in range(size)])  101 us
    unnamed x40, local copies, waits for them, and re-layouts  33.3 us
    all_gather x1, blocking collectives, on_device(): lax.all_gather(pivot_masked[:, :, :panel_width], 'prow', axis=1, tiled=True)  32.2 us
    ppermute x16, starting transfers between devices, ring(): lax.ppermute(value, axis, [(i, (i + step) % size) for i in range(size)])  27.6 us
    dot_general x4, matrix products, on_device(): jnp.dot(lower_rel, stacked, preferred_element_type=jnp.float32)  22.9 us
    dot_general x4, matrix products, on_device(): jnp.dot(pivot_rel, first_rel, preferred_element_type=jnp.float32)  10.1 us
  transfers between devices with their start and end apart: 22, of which 12 were waited for; matrix products, arithmetic and copies ran while one was open for 15% of the time, Pallas kernels for 0%

profile of v1, /device:TPU:0, one launch (start us, length us, event | category | flops | bytes accessed | tf_op | source)
XLA Modules:
  0.0 440.5 jit_solution(11904889417108722127)
XLA Ops:
  7.2 0.7 convert_bitcast_fusion
  8.1 2.7 bitcast_multiply_fusion.1
  10.8 4.4 fusion.41
  15.2 2.0 collective-permute-start.7
  17.2 2.1 collective-permute-start.6
  19.3 32.2 %all_gather.3 = bf16[2,256,512]{2,1,0:T(8,128)(2,1)S(1)} all-gather(bf16[2,64,512]{2,1,0:T(8,128)(2,1)S(1)} %slice.159), channel_id=1, replica_groups=mesh['layer'=16,'prow'=4,'pcol'=2] {'prow'}, dimensions={1}, use_global_device_ids=true | all-gather | bytes 655360 | tf_op jit(solution)/shard_map/all_gather | solution.py:45
  51.7 1.3 collective-permute-start.5
  53.1 2.7 mul.34
  55.8 10.4 %copy.9 = bf16[64,8,64,256]{3,1,2,0:T(8,128)(2,1)S(1)} copy(bf16[64,8,64,256]{3,2,1,0:T(8,128)(2,1)S(1)} %bitcast.79) | data formatting | bytes 33554432
  66.3 8.3 %bitcast_multiply_fusion = bf16[512,16384]{1,0:T(8,128)(2,1)S(1)} fusion(bf16[512,16384]{1,0:T(8,128)(2,1)S(1)} %bitcast.78, bf16[1,512,16384]{2,1,0:T(8,128)(2,1)} %param.7), kind=kLoop, calls=%fused_computation | loop fusion | flops 8388608 | bytes 50331648 | tf_op jit(solution)/shard_map/mul | solution.py:33
  74.6 5.7 %copy-done = bf16[512,16384]{1,0:T(8,128)(2,1)} copy-done((bf16[512,16384]{1,0:T(8,128)(2,1)}, bf16[512,16384]{1,0:T(8,128)(2,1)S(1)}, u32[]{:S(2)}) %copy-start) | copy-done | bytes 16777240
  80.6 1.4 convolution_convert_fusion
  82.0 0.8 pad_maximum_fusion
  82.9 2.1 collective-permute-start
  85.5 0.5 collective-permute-done
  86.2 1.6 collective-permute-start.8
  88.3 1.8 collective-permute-start.9
  90.2 11.8 %collective-permute-done.8 = bf16[2,32,4096]{2,1,0:T(8,128)(2,1)S(1)} collective-permute-done((bf16[2,32,4096]{2,1,0:T(8,128)(2,1)S(1)}, bf16[2,32,4096]{2,1,0:T(8,128)(2,1)S(1)}, u32[]{:S(2)}, u32[]{:S(2)}) %collective-permute-start.8) | collective-permute-done | bytes 524320 | tf_op jit(solution)/shard_map/ppermute | solution.py:10
  102.0 1.0 collective-permute-done.9
  103.3 0.7 fusion.14
  104.1 1.3 copy-done.5
  105.4 5.7 %select_convert_fusion.2 = bf16[512,4096]{1,0:T(8,128)(2,1)} fusion(bf16[512,16384]{1,0:T(8,128)(2,1)} %copy-done, bf16[256,4096]{1,0:T(8,128)(2,1)S(1)} %fusion.14, bf16[256,4096]{1,0:T(8,128)(2,1)S(1)} %slice_bitcast_fusion.5, pred[4096]{0:T(1024)(128)(4,1)S(1)} %add_compare_fusion.2, bf16[512,256]{0,1:T(8,128)(2,1)S(1)} %get-tuple-element.19, ...), kind=kOutput, calls=%fused_computation.3 | convolution fusion | flops 2165309440 | bytes 13111296 | tf_op jit(solution)/shard_map/dot_general | solution.py:92
  111.7 2.8 collective-permute-start.10
  114.5 23.4 %collective-permute-done.11 = bf16[2,64,4096]{2,1,0:T(8,128)(2,1)S(1)} collective-permute-done((bf16[2,64,4096]{2,1,0:T(8,128)(2,1)}, bf16[2,64,4096]{2,1,0:T(8,128)(2,1)S(1)}, u32[]{:S(2)}, u32[]{:S(2)}) %collective-permute-start.11) | collective-permute-done | bytes 1048608 | tf_op jit(solution)/shard_map/ppermute | solution.py:10
  138.0 3.5 collective-permute-start.13
  141.5 1.1 constant_dynamic-update-slice_fusion.13
  142.5 9.7 %collective-permute-done.12 = bf16[2,32,4096]{2,1,0:T(8,128)(2,1)S(1)} collective-permute-done((bf16[2,32,4096]{2,1,0:T(8,128)(2,1)S(1)}, bf16[2,32,4096]{2,1,0:T(8,128)(2,1)S(1)}, u32[]{:S(2)}, u32[]{:S(2)}) %collective-permute-start.12) | collective-permute-done | bytes 524320 | tf_op jit(solution)/shard_map/ppermute | solution.py:10
  152.3 0.8 constant_dynamic-update-slice_fusion.12
  153.1 0.8 constant_dynamic-update-slice_fusion.11
  154.0 1.1 constant_dynamic-update-slice_fusion.10
  155.0 3.2 fusion.13
  158.2 0.5 copy-done.3
  158.9 1.2 copy-done.6
  160.0 5.7 %select_convert_fusion.1 = bf16[512,4096]{1,0:T(8,128)(2,1)} fusion(bf16[512,16384]{1,0:T(8,128)(2,1)} %copy-done, bf16[256,4096]{1,0:T(8,128)(2,1)S(1)} %fusion.13, bf16[256,4096]{1,0:T(8,128)(2,1)S(1)} %slice_bitcast_fusion.3, pred[4096]{0:T(1024)(128)(4,1)S(1)} %add_compare_fusion.1, bf16[512,256]{0,1:T(8,128)(2,1)S(1)} %get-tuple-element.19, ...), kind=kOutput, calls=%fused_computation.2 | convolution fusion | flops 2165309440 | bytes 13111296 | tf_op jit(solution)/shard_map/dot_general | solution.py:92
  165.9 3.2 collective-permute-start.14
  169.1 21.4 %collective-permute-done.15 = bf16[2,64,4096]{2,1,0:T(8,128)(2,1)S(1)} collective-permute-done((bf16[2,64,4096]{2,1,0:T(8,128)(2,1)}, bf16[2,64,4096]{2,1,0:T(8,128)(2,1)S(1)}, u32[]{:S(2)}, u32[]{:S(2)}) %collective-permute-start.15) | collective-permute-done | bytes 1048608 | tf_op jit(solution)/shard_map/ppermute | solution.py:10
  190.8 3.3 collective-permute-start.17
  194.0 1.1 constant_dynamic-update-slice_fusion.18
  195.1 7.9 %collective-permute-done.16 = bf16[2,32,4096]{2,1,0:T(8,128)(2,1)S(1)} collective-permute-done((bf16[2,32,4096]{2,1,0:T(8,128)(2,1)S(1)}, bf16[2,32,4096]{2,1,0:T(8,128)(2,1)S(1)}, u32[]{:S(2)}, u32[]{:S(2)}) %collective-permute-start.16) | collective-permute-done | bytes 524320 | tf_op jit(solution)/shard_map/ppermute | solution.py:10
  203.1 0.8 constant_dynamic-update-slice_fusion.17
  203.9 0.9 constant_dynamic-update-slice_fusion.16
  204.8 1.1 constant_dynamic-update-slice_fusion.15
  205.9 3.1 fusion.12
  209.6 1.2 copy-done.7
  210.7 5.7 %select_convert_fusion = bf16[512,4096]{1,0:T(8,128)(2,1)} fusion(bf16[512,16384]{1,0:T(8,128)(2,1)} %copy-done, bf16[256,4096]{1,0:T(8,128)(2,1)S(1)} %fusion.12, bf16[256,4096]{1,0:T(8,128)(2,1)S(1)} %slice_bitcast_fusion.1, pred[4096]{0:T(1024)(128)(4,1)S(1)} %add_compare_fusion, bf16[512,256]{0,1:T(8,128)(2,1)S(1)} %get-tuple-element.19, ...), kind=kOutput, calls=%fused_computation.1 | convolution fusion | flops 2165309440 | bytes 13111296 | tf_op jit(solution)/shard_map/dot_general | solution.py:92
  216.5 1.2 copy-done.9
  217.7 3.2 collective-permute-start.1
  220.9 19.9 %collective-permute-done.2 = bf16[2,64,4096]{2,1,0:T(8,128)(2,1)S(1)} collective-permute-done((bf16[2,64,4096]{2,1,0:T(8,128)(2,1)S(1)}, bf16[2,64,4096]{2,1,0:T(8,128)(2,1)S(1)}, u32[]{:S(2)}, u32[]{:S(2)}) %collective-permute-start.2) | collective-permute-done | bytes 1048608 | tf_op jit(solution)/shard_map/ppermute | solution.py:10
  241.0 3.3 collective-permute-start.4
  244.3 1.1 constant_dynamic-update-slice_fusion.3
  245.3 6.3 %collective-permute-done.3 = bf16[2,32,4096]{2,1,0:T(8,128)(2,1)S(1)} collective-permute-done((bf16[2,32,4096]{2,1,0:T(8,128)(2,1)S(1)}, bf16[2,32,4096]{2,1,0:T(8,128)(2,1)S(1)}, u32[]{:S(2)}, u32[]{:S(2)}) %collective-permute-start.3) | collective-permute-done | bytes 524320 | tf_op jit(solution)/shard_map/ppermute | solution.py:10
  251.7 0.8 constant_dynamic-update-slice_fusion.2
  252.5 0.9 constant_dynamic-update-slice_fusion.1
  253.4 1.1 constant_dynamic-update-slice_fusion
  254.4 3.1 fusion.15
  257.5 0.5 copy-done.1
  258.2 1.2 copy-done.8
  259.4 5.8 %select_convert_fusion.3 = bf16[512,4096]{1,0:T(8,128)(2,1)} fusion(bf16[512,16384]{1,0:T(8,128)(2,1)} %copy-done, bf16[256,4096]{1,0:T(8,128)(2,1)S(1)} %fusion.15, bf16[256,4096]{1,0:T(8,128)(2,1)S(1)} %slice_bitcast_fusion.7, pred[4096]{0:T(1024)(128)(4,1)S(1)} %add_compare_fusion.3, bf16[512,256]{0,1:T(8,128)(2,1)S(1)} %get-tuple-element.19, ...), kind=kOutput, calls=%fused_computation.4 | convolution fusion | flops 2165309440 | bytes 13111296 | tf_op jit(solution)/shard_map/dot_general | solution.py:92
  265.2 1.0 copy.8
  266.9 1.5 maximum_bitcast_fusion
  268.4 2.3 reduce-scatter.9.cloned.1.call-done
  270.7 80.2 %reduce-scatter.11.cloned.1.call-done = bf16[32,4096]{1,0:T(8,128)(2,1)} async-done(((bf16[512,4096]{1,0:T(8,128)(2,1)}), bf16[32,4096]{1,0:T(8,128)(2,1)}) %reduce-scatter.11.cloned.1.call-update) | async-done | bytes 262160 | tf_op jit(solution)/shard_map/reduce_scatter | solution.py:97
  350.9 80.5 %reduce-scatter.5.cloned.1.call-done = bf16[32,4096]{1,0:T(8,128)(2,1)} async-done(((bf16[512,4096]{1,0:T(8,128)(2,1)}), bf16[32,4096]{1,0:T(8,128)(2,1)}) %reduce-scatter.5.cloned.1.call-update) | async-done | bytes 262160 | tf_op jit(solution)/shard_map/reduce_scatter | solution.py:97
  431.4 2.6 maximum_convert_fusion
  (81 shorter events, 5.0 us)
Async XLA Ops:
  7.2 261.2 %reduce-scatter.7.cloned.1.call-start = ((), (), s32[]{:S(2)}) async-start(), calls=%async_computation.5 | async-start | bytes 4456448 | tf_op jit(solution)/shard_map/reduce_scatter | solution.py:97
  10.8 40.8 %copy-start.10 = (bf16[1,2,256,256]{3,2,1,0:T(8,128)(2,1)S(1)}, bf16[1,2,256,256]{3,2,1,0:T(8,128)(2,1)}, u32[]{:S(2)}) copy-start(bf16[1,2,256,256]{3,2,1,0:T(8,128)(2,1)} %param.9) | copy-start | bytes 786436
  10.8 42.3 %copy-start.11 = (s32[1,2,64]{2,1,0:T(2,128)S(1)}, s32[1,2,64]{2,1,0:T(2,128)}, u32[]{:S(2)}) copy-start(s32[1,2,64]{2,1,0:T(2,128)} %param.10) | copy-start | bytes 1540
  15.2 71.0 %collective-permute-start.7 = (bf16[2,64,4096]{2,1,0:T(8,128)(2,1)}, bf16[2,64,4096]{2,1,0:T(8,128)(2,1)S(1)}, u32[]{:S(2)}, u32[]{:S(2)}) collective-permute-start(bf16[2,64,4096]{2,1,0:T(8,128)(2,1)} %get-tuple-element.14), channel_id=1, source_target_pairs={{0,2},{2,4},{4,6},{6,0},{1,3},{3,5},{5,7},{7,1},{8,10},{10,12},{12... | collective-permute-start | bytes 3145736 | tf_op jit(solution)/shard_map/ppermute | solution.py:10
  17.2 71.1 %collective-permute-start.6 = (bf16[2,64,4096]{2,1,0:T(8,128)(2,1)}, bf16[2,64,4096]{2,1,0:T(8,128)(2,1)S(1)}, u32[]{:S(2)}, u32[]{:S(2)}) collective-permute-start(bf16[2,64,4096]{2,1,0:T(8,128)(2,1)} %get-tuple-element.14), channel_id=1, source_target_pairs={{0,6},{2,0},{4,2},{6,4},{1,7},{3,1},{5,3},{7,5},{8,14},{10,8},{12,... | collective-permute-start | bytes 3145736 | tf_op jit(solution)/shard_map/ppermute | solution.py:10
  51.7 33.2 %collective-permute-start.5 = (bf16[256,256]{1,0:T(8,128)(2,1)S(1)}, bf16[256,256]{1,0:T(8,128)(2,1)S(1)}, u32[]{:S(2)}, u32[]{:S(2)}) collective-permute-start(bf16[256,256]{1,0:T(8,128)(2,1)S(1)} %convolution_convert_fusion.2), channel_id=1, source_target_pairs={{0,1},{2,3},{4,5},{6,7},{8,9},{10,11},{12,13},{14,15},{16,17},{18,... | collective-permute-start | bytes 393224 | tf_op jit(solution)/shard_map/ppermute | solution.py:62
  74.6 5.8 %copy-start = (bf16[512,16384]{1,0:T(8,128)(2,1)}, bf16[512,16384]{1,0:T(8,128)(2,1)S(1)}, u32[]{:S(2)}) copy-start(bf16[512,16384]{1,0:T(8,128)(2,1)S(1)} %bitcast_multiply_fusion) | copy-start | bytes 50331652
  82.9 3.1 collective-permute-start
  84.9 5.2 %copy-start.4 = (bf16[2,256,4096]{2,1,0:T(8,128)(2,1)S(1)}, bf16[2,256,4096]{2,1,0:T(8,128)(2,1)}, u32[]{:S(2)}) copy-start(bf16[2,256,4096]{2,1,0:T(8,128)(2,1)} %get-tuple-element.9) | copy-start | bytes 12582916
  86.2 15.7 %collective-permute-start.8 = (bf16[2,32,4096]{2,1,0:T(8,128)(2,1)S(1)}, bf16[2,32,4096]{2,1,0:T(8,128)(2,1)S(1)}, u32[]{:S(2)}, u32[]{:S(2)}) collective-permute-start(bf16[2,32,4096]{2,1,0:T(8,128)(2,1)S(1)} %slice.173), channel_id=1, source_target_pairs={{0,2},{2,4},{4,6},{6,0},{1,3},{3,5},{5,7},{7,1},{8,10},{10,12},{12... | collective-permute-start | bytes 1572872 | tf_op jit(solution)/shard_map/ppermute | solution.py:10
  88.3 14.7 %collective-permute-start.9 = (bf16[2,32,4096]{2,1,0:T(8,128)(2,1)S(1)}, bf16[2,32,4096]{2,1,0:T(8,128)(2,1)S(1)}, u32[]{:S(2)}, u32[]{:S(2)}) collective-permute-start(bf16[2,32,4096]{2,1,0:T(8,128)(2,1)S(1)} %slice.174), channel_id=1, source_target_pairs={{0,6},{2,0},{4,2},{6,4},{1,7},{3,1},{5,3},{7,5},{8,14},{10,8},{12,... | collective-permute-start | bytes 1572872 | tf_op jit(solution)/shard_map/ppermute | solution.py:10
  104.1 1.3 copy-start.5
  111.1 159.6 %reduce-scatter.9.cloned.1.call-start = ((), (), s32[]{:S(2)}) async-start(), calls=%async_computation.6 | async-start | bytes 4456448 | tf_op jit(solution)/shard_map/reduce_scatter | solution.py:97
  111.2 26.7 %collective-permute-start.11 = (bf16[2,64,4096]{2,1,0:T(8,128)(2,1)}, bf16[2,64,4096]{2,1,0:T(8,128)(2,1)S(1)}, u32[]{:S(2)}, u32[]{:S(2)}) collective-permute-start(bf16[2,64,4096]{2,1,0:T(8,128)(2,1)} %get-tuple-element.13), channel_id=1, source_target_pairs={{0,2},{2,4},{4,6},{6,0},{1,3},{3,5},{5,7},{7,1},{8,10},{10,12},{12... | collective-permute-start | bytes 3145736 | tf_op jit(solution)/shard_map/ppermute | solution.py:10
  111.7 26.3 %collective-permute-start.10 = (bf16[2,64,4096]{2,1,0:T(8,128)(2,1)}, bf16[2,64,4096]{2,1,0:T(8,128)(2,1)S(1)}, u32[]{:S(2)}, u32[]{:S(2)}) collective-permute-start(bf16[2,64,4096]{2,1,0:T(8,128)(2,1)} %get-tuple-element.13), channel_id=1, source_target_pairs={{0,6},{2,0},{4,2},{6,4},{1,7},{3,1},{5,3},{7,5},{8,14},{10,8},{12,... | collective-permute-start | bytes 3145736 | tf_op jit(solution)/shard_map/ppermute | solution.py:10
  137.9 14.4 %collective-permute-start.12 = (bf16[2,32,4096]{2,1,0:T(8,128)(2,1)S(1)}, bf16[2,32,4096]{2,1,0:T(8,128)(2,1)S(1)}, u32[]{:S(2)}, u32[]{:S(2)}) collective-permute-start(bf16[2,32,4096]{2,1,0:T(8,128)(2,1)S(1)} %slice.179), channel_id=1, source_target_pairs={{0,2},{2,4},{4,6},{6,0},{1,3},{3,5},{5,7},{7,1},{8,10},{10,12},{12... | collective-permute-start | bytes 1572872 | tf_op jit(solution)/shard_map/ppermute | solution.py:10
  138.0 15.1 %collective-permute-start.13 = (bf16[2,32,4096]{2,1,0:T(8,128)(2,1)S(1)}, bf16[2,32,4096]{2,1,0:T(8,128)(2,1)S(1)}, u32[]{:S(2)}, u32[]{:S(2)}) collective-permute-start(bf16[2,32,4096]{2,1,0:T(8,128)(2,1)S(1)} %slice.180), channel_id=1, source_target_pairs={{0,6},{2,0},{4,2},{6,4},{1,7},{3,1},{5,3},{7,5},{8,14},{10,8},{12,... | collective-permute-start | bytes 1572872 | tf_op jit(solution)/shard_map/ppermute | solution.py:10
  155.0 3.7 copy-start.3
  158.7 1.3 copy-start.6
  165.8 185.1 %reduce-scatter.11.cloned.1.call-start = ((), (), s32[]{:S(2)}) async-start(), calls=%async_computation.7 | async-start | bytes 4456448 | tf_op jit(solution)/shard_map/reduce_scatter | solution.py:97
  165.8 24.7 %collective-permute-start.15 = (bf16[2,64,4096]{2,1,0:T(8,128)(2,1)}, bf16[2,64,4096]{2,1,0:T(8,128)(2,1)S(1)}, u32[]{:S(2)}, u32[]{:S(2)}) collective-permute-start(bf16[2,64,4096]{2,1,0:T(8,128)(2,1)} %get-tuple-element.12), channel_id=1, source_target_pairs={{0,2},{2,4},{4,6},{6,0},{1,3},{3,5},{5,7},{7,1},{8,10},{10,12},{12... | collective-permute-start | bytes 3145736 | tf_op jit(solution)/shard_map/ppermute | solution.py:10
  165.9 24.8 %collective-permute-start.14 = (bf16[2,64,4096]{2,1,0:T(8,128)(2,1)}, bf16[2,64,4096]{2,1,0:T(8,128)(2,1)S(1)}, u32[]{:S(2)}, u32[]{:S(2)}) collective-permute-start(bf16[2,64,4096]{2,1,0:T(8,128)(2,1)} %get-tuple-element.12), channel_id=1, source_target_pairs={{0,6},{2,0},{4,2},{6,4},{1,7},{3,1},{5,3},{7,5},{8,14},{10,8},{12,... | collective-permute-start | bytes 3145736 | tf_op jit(solution)/shard_map/ppermute | solution.py:10
  190.6 12.5 %collective-permute-start.16 = (bf16[2,32,4096]{2,1,0:T(8,128)(2,1)S(1)}, bf16[2,32,4096]{2,1,0:T(8,128)(2,1)S(1)}, u32[]{:S(2)}, u32[]{:S(2)}) collective-permute-start(bf16[2,32,4096]{2,1,0:T(8,128)(2,1)S(1)} %slice.185), channel_id=1, source_target_pairs={{0,2},{2,4},{4,6},{6,0},{1,3},{3,5},{5,7},{7,1},{8,10},{10,12},{12... | collective-permute-start | bytes 1572872 | tf_op jit(solution)/shard_map/ppermute | solution.py:10
  190.8 13.1 %collective-permute-start.17 = (bf16[2,32,4096]{2,1,0:T(8,128)(2,1)S(1)}, bf16[2,32,4096]{2,1,0:T(8,128)(2,1)S(1)}, u32[]{:S(2)}, u32[]{:S(2)}) collective-permute-start(bf16[2,32,4096]{2,1,0:T(8,128)(2,1)S(1)} %slice.186), channel_id=1, source_target_pairs={{0,6},{2,0},{4,2},{6,4},{1,7},{3,1},{5,3},{7,5},{8,14},{10,8},{12,... | collective-permute-start | bytes 1572872 | tf_op jit(solution)/shard_map/ppermute | solution.py:10
  205.9 3.5 copy-start.2
  209.4 1.3 copy-start.7
  216.5 1.2 copy-start.9
  216.5 214.9 %reduce-scatter.5.cloned.1.call-start = ((), (), s32[]{:S(2)}) async-start(), calls=%async_computation.4 | async-start | bytes 4456448 | tf_op jit(solution)/shard_map/reduce_scatter | solution.py:97
  217.7 23.1 %collective-permute-start.2 = (bf16[2,64,4096]{2,1,0:T(8,128)(2,1)S(1)}, bf16[2,64,4096]{2,1,0:T(8,128)(2,1)S(1)}, u32[]{:S(2)}, u32[]{:S(2)}) collective-permute-start(bf16[2,64,4096]{2,1,0:T(8,128)(2,1)S(1)} %copy-done.9), channel_id=1, source_target_pairs={{0,2},{2,4},{4,6},{6,0},{1,3},{3,5},{5,7},{7,1},{8,10},{10,12},{12... | collective-permute-start | bytes 3145736 | tf_op jit(solution)/shard_map/ppermute | solution.py:10
  217.7 23.2 %collective-permute-start.1 = (bf16[2,64,4096]{2,1,0:T(8,128)(2,1)S(1)}, bf16[2,64,4096]{2,1,0:T(8,128)(2,1)S(1)}, u32[]{:S(2)}, u32[]{:S(2)}) collective-permute-start(bf16[2,64,4096]{2,1,0:T(8,128)(2,1)S(1)} %copy-done.9), channel_id=1, source_target_pairs={{0,6},{2,0},{4,2},{6,4},{1,7},{3,1},{5,3},{7,5},{8,14},{10,8},{12,... | collective-permute-start | bytes 3145736 | tf_op jit(solution)/shard_map/ppermute | solution.py:10
  240.8 10.8 %collective-permute-start.3 = (bf16[2,32,4096]{2,1,0:T(8,128)(2,1)S(1)}, bf16[2,32,4096]{2,1,0:T(8,128)(2,1)S(1)}, u32[]{:S(2)}, u32[]{:S(2)}) collective-permute-start(bf16[2,32,4096]{2,1,0:T(8,128)(2,1)S(1)} %slice.165), channel_id=1, source_target_pairs={{0,2},{2,4},{4,6},{6,0},{1,3},{3,5},{5,7},{7,1},{8,10},{10,12},{12... | collective-permute-start | bytes 1572872 | tf_op jit(solution)/shard_map/ppermute | solution.py:10
  241.0 11.5 %collective-permute-start.4 = (bf16[2,32,4096]{2,1,0:T(8,128)(2,1)S(1)}, bf16[2,32,4096]{2,1,0:T(8,128)(2,1)S(1)}, u32[]{:S(2)}, u32[]{:S(2)}) collective-permute-start(bf16[2,32,4096]{2,1,0:T(8,128)(2,1)S(1)} %slice.166), channel_id=1, source_target_pairs={{0,6},{2,0},{4,2},{6,4},{1,7},{3,1},{5,3},{7,5},{8,14},{10,8},{12,... | collective-permute-start | bytes 1572872 | tf_op jit(solution)/shard_map/ppermute | solution.py:10
  254.4 3.6 copy-start.1
  258.1 1.3 copy-start.8
  265.2 1.0 slice-start
  265.2 1.3 slice-start.1
  265.2 1.5 slice-start.2
  265.2 1.7 slice-start.3
Sparse Core Ops, SparseCore 0:
  111.2 78.7 reduce-scatter.6
  193.7 76.9 reduce-scatter.8
  274.0 76.8 reduce-scatter.10
  354.5 76.8 reduce-scatter.4

commit v2 on v0

--- a/solution.py
+++ b/solution.py
@@ -4,9 +4,18 @@
 from jax.sharding import PartitionSpec as P
 
 
-def spread(value, axis, root):
-    mine = lax.axis_index(axis) == root
-    return lax.psum(jnp.where(mine, value, jnp.zeros_like(value)), axis)
+def ring(value, axis, size, step):
+    return lax.ppermute(value, axis, [(i, (i + step) % size) for i in range(size)])
+
+
+def gather_relative(value, axis, size):
+    from_prev = ring(value, axis, size, 1)
+    from_next = ring(value, axis, size, -1)
+    half = value.shape[1] // 2
+    far_lo = ring(from_prev[:, :half], axis, size, 1)
+    far_hi = ring(from_next[:, half:], axis, size, -1)
+    far = jnp.concatenate([far_lo, far_hi], 1)
+    return jnp.concatenate([value, from_next, far, from_prev], 1)
 
 
 def on_device(front, pivots, inverses, slab_pattern, pivot_pattern):
@@ -26,26 +35,20 @@
     first_inverse = inverses[0, 0]
     second_inverse = inverses[0, 1]
     row_offset = lax.axis_index("prow") * own_rows
+    pcol = lax.axis_index("pcol")
+    n_prow = lax.axis_size("prow")
+    n_pcol = lax.axis_size("pcol")
+    assert n_prow == 4
     gathered = lax.all_gather(pivot_masked, "prow", axis=1, tiled=True)
-    panel_cols = spread(
-        jnp.concatenate(
-            [masked[:, :panel_width], gathered[0][:, :panel_width], gathered[1][:, :panel_width]], 0
-        ),
-        "pcol",
-        0,
+    panel = jnp.roll(
+        gather_relative(pivot_masked[:, :, :panel_width], "prow", n_prow), row_offset, axis=1
     )
-    front_cols = panel_cols[:row_count]
-    pivot_cols = panel_cols[row_count : row_count + block_size]
-    second_cols = panel_cols[row_count + block_size :]
+    front_cols = masked[:, :panel_width]
+    pivot_cols = panel[0]
+    second_cols = panel[1]
     lower_pivot = jnp.dot(
         second_cols[:, :block_size], first_inverse, preferred_element_type=jnp.float32
     ).astype(jnp.bfloat16)
-    upper_first = gathered[0]
-    upper_second = (
-        gathered[1].astype(jnp.float32)
-        - jnp.dot(lower_pivot, upper_first, preferred_element_type=jnp.float32)
-    ).astype(jnp.bfloat16)
-    upper_own = lax.dynamic_slice_in_dim(upper_second, row_offset, own_rows, 0)
     lower_first = jnp.dot(
         front_cols[:, :block_size], first_inverse, preferred_element_type=jnp.float32
     ).astype(jnp.bfloat16)
@@ -59,6 +62,16 @@
         jnp.bfloat16
     )
     lower_panel = jnp.concatenate([lower_first, lower_second], 1)
+    sent = lax.ppermute((lower_panel, lower_pivot), "pcol", [(0, i) for i in range(1, n_pcol)])
+    on_root = pcol == 0
+    lower_panel = jnp.where(on_root, lower_panel, sent[0])
+    lower_pivot = jnp.where(on_root, lower_pivot, sent[1])
+    upper_first = gathered[0]
+    upper_second = (
+        gathered[1].astype(jnp.float32)
+        - jnp.dot(lower_pivot, upper_first, preferred_element_type=jnp.float32)
+    ).astype(jnp.bfloat16)
+    upper_own = lax.dynamic_slice_in_dim(upper_second, row_offset, own_rows, 0)
     stacked = jnp.concatenate([upper_first, upper_second], 0)
     col_index = lax.axis_index("pcol") * col_count + jnp.arange(col_count, dtype=jnp.int32)
     retained = col_index >= panel_width

time: 363 us -> 332 us (0.915)
  waiting for transfers between devices: 262 us -> 217 us
  starting transfers between devices: 0.12 us -> 10.3 us
    psum x1 -> x0, waiting for transfers between devices: 26.2 us -> none  [spread(): return lax.psum(jnp.where(mine, value, jnp.zeros_like(value)), axis)]
    all_gather x1, waiting for transfers between devices: 127 us -> 106 us  [on_device(): gathered = lax.all_gather(pivot_masked, 'prow', axis=1, tiled=True)]
    ppermute x0 -> x6, starting transfers between devices: none -> 10.2 us  [the longest x4 7.57 us: ring(): lax.ppermute(value, axis, [(i, (i + step) % size) for i in range(size)])]
    ppermute x0 -> x6, waiting for transfers between devices: none -> 3.79 us  [the longest x4 3.78 us: ring(): lax.ppermute(value, axis, [(i, (i + step) % size) for i in range(size)])]
    squeeze x1 -> x2, local copies, waits for them, and re-layouts: 6.73 us -> 7.52 us  [the longest x1 7.47 us: on_device(): upper_first = gathered[0]]
    unnamed x10 -> x16, local copies, waits for them, and re-layouts: 20.5 us -> 20.4 us
  transfers between devices with their start and end apart: 3 -> 8, of which waited for: 3 -> 3; matrix products, arithmetic and copies ran while one was open for 8% -> 16% of each run, Pallas kernels for 0% -> 0%
where the time goes in v2:
time: 332 us; the launch traced here: 331 us
  waiting for transfers between devices  217 us (65%)
  local copies, waits for them, and re-layouts  34.6 us (10%)
  matrix products  33 us (10%)
  other arithmetic  21.5 us (6%)
  between operations  14.2 us (4%)
  starting transfers between devices  10.3 us (3%)
    reduce_scatter x1, waiting for transfers between devices, on_device(): lax.psum_scatter(schur_rows.astype(jnp.bfloat16), 'layer', scatter_dimens...  107 us
    all_gather x1, waiting for transfers between devices, on_device(): gathered = lax.all_gather(pivot_masked, 'prow', axis=1, tiled=True)  106 us
    dot_general x1, matrix products, on_device(): jnp.dot(lower_panel, stacked, preferred_element_type=jnp.float32)  21.9 us
    unnamed x16, local copies, waits for them, and re-layouts  20.4 us
    mul x1, other arithmetic, on_device(): front[0]  12.5 us
    dot_general x1, matrix products, on_device(): jnp.dot(lower_pivot, upper_first, preferred_element_type=jnp.float32)  9.17 us
    ppermute x4, starting transfers between devices, ring(): lax.ppermute(value, axis, [(i, (i + step) % size) for i in range(size)])  7.57 us
    squeeze x1, local copies, waits for them, and re-layouts, on_device(): upper_first = gathered[0]  7.47 us
  transfers between devices with their start and end apart: 8, of which 3 were waited for; matrix products, arithmetic and copies ran while one was open for 16% of the time, Pallas kernels for 0%

profile of v2, /device:TPU:0, one launch (start us, length us, event | category | flops | bytes accessed | tf_op | source)
XLA Modules:
  0.0 330.8 jit_solution(8461802693359188923)
XLA Ops:
  7.2 0.0 all-gather.2.cloned.1.call-start
  7.2 0.7 convert_bitcast_fusion
  7.9 0.1 broadcast_bitcast_fusion
  8.0 0.1 copy.10
  8.1 4.8 %bitcast_multiply_fusion.1 = bf16[2,64,16384]{2,1,0:T(8,128)(2,1)} fusion(bf16[1,2,64,16384]{3,2,1,0:T(8,128)(2,1)} %param.6, bf16[2,16384]{1,0:T(2,128)(2,1)S(1)} %bitcast.44), kind=kLoop, calls=%fused_computation.9 | loop fusion | flops 2097152 | bytes 8454144 | tf_op jit(solution)/shard_map/mul | solution.py:32
  12.8 0.0 all-gather.2.cloned.1.call-update
  12.9 0.0 reduce-scatter.2.cloned.1.call-start
  12.9 0.9 fusion.21
  13.9 4.2 %collective-permute-start = (bf16[2,64,512]{2,1,0:T(8,128)(2,1)S(1)}, bf16[2,64,512]{2,1,0:T(8,128)(2,1)S(1)}, u32[]{:S(2)}, u32[]{:S(2)}) collective-permute-start(bf16[2,64,512]{2,1,0:T(8,128)(2,1)S(1)} %get-tuple-element.6), channel_id=1, source_target_pairs={{0,6},{2,0},{4,2},{6,4},{1,7},{3,1},{5,3},{7,5},{8,14},{10,8},{12,... | collective-permute-start | bytes 393224 | tf_op jit(solution)/shard_map/ppermute | solution.py:8
  18.0 0.0 collective-permute-start.1
  18.0 0.7 convert_bitcast_fusion.1
  18.7 2.7 mul.31
  21.5 12.4 %copy.9 = bf16[64,8,64,256]{3,1,2,0:T(8,128)(2,1)} copy(bf16[64,8,64,256]{3,2,1,0:T(8,128)(2,1)S(1)} %bitcast.43) | data formatting | bytes 33554432
  33.9 0.0 copy-start.1
  33.9 12.5 %bitcast_multiply_fusion = bf16[512,16384]{1,0:T(8,128)(2,1)S(1)} fusion(bf16[512,16384]{1,0:T(8,128)(2,1)} %bitcast.42, bf16[1,512,16384]{2,1,0:T(8,128)(2,1)} %param.5), kind=kLoop, calls=%fused_computation.6 | loop fusion | flops 8388608 | bytes 50331648 | tf_op jit(solution)/shard_map/mul | solution.py:28
  46.4 0.0 copy-start
  46.4 5.8 %copy-done = bf16[512,16384]{1,0:T(8,128)(2,1)} copy-done((bf16[512,16384]{1,0:T(8,128)(2,1)}, bf16[512,16384]{1,0:T(8,128)(2,1)S(1)}, u32[]{:S(2)}) %copy-start) | copy-done | bytes 16777240
  52.2 0.0 copy-done.1
  52.2 0.3 convolution_convert_fusion.1
  52.5 0.0 collective-permute-done.1
  52.6 0.3 collective-permute-start.2
  52.9 0.0 collective-permute-done
  52.9 3.1 collective-permute-start.3
  56.0 3.8 %collective-permute-done.2 = bf16[2,32,512]{2,1,0:T(8,128)(2,1)S(1)} collective-permute-done((bf16[2,32,512]{2,1,0:T(8,128)(2,1)S(1)}, bf16[2,32,512]{2,1,0:T(8,128)(2,1)S(1)}, u32[]{:S(2)}, u32[]{:S(2)}) %collective-permute-start.2) | collective-permute-done | bytes 65568 | tf_op jit(solution)/shard_map/ppermute | solution.py:8
  59.7 0.0 collective-permute-done.3
  59.8 0.9 constant_dynamic-update-slice_fusion.4
  60.8 0.2 convolution_convert_fusion.2
  61.0 1.3 collective-permute-start.5
  62.3 1.4 convolution_convert_fusion
  63.8 1.3 collective-permute-start.4
  65.1 105.9 %all-gather.2.cloned.1.call-done = bf16[2,256,16384]{2,1,0:T(8,128)(2,1)} async-done(((bf16[2,64,16384]{2,1,0:T(8,128)(2,1)}), bf16[2,256,16384]{2,1,0:T(8,128)(2,1)}) %all-gather.2.cloned.1.call-update) | async-done | bytes 16777232 | tf_op jit(solution)/shard_map/all_gather | solution.py:42
  171.1 7.5 %slice_bitcast_fusion.1 = bf16[256,16384]{1,0:T(8,128)(2,1)} fusion(bf16[2,256,16384]{2,1,0:T(8,128)(2,1)} %all-gather.2.cloned.1.call-done), kind=kLoop, calls=%fused_computation.8 | loop fusion | bytes 16777216 | tf_op jit(solution)/shard_map/squeeze | solution.py:69
  178.5 0.0 collective-permute-done.5
  178.5 9.2 %fusion = bf16[256,16384]{1,0:T(8,128)(2,1)} fusion(bf16[2,256,16384]{2,1,0:T(8,128)(2,1)} %all-gather.2.cloned.1.call-done, bf16[256,256]{1,0:T(8,128)(2,1)S(1)} %convolution_convert_fusion.2, bf16[256,256]{1,0:T(8,128)(2,1)S(1)} %collective-permute-done.5, pred[]{:T(512)S(6)} %eq.6), kind=kOutput, calls=%fused_computation.2 | convolution fusion | flops 2160132096 | bytes 25427968 | tf_op jit(solution)/shard_map/dot_general | solution.py:72
  187.7 0.0 collective-permute-done.4
  187.7 21.9 %select_convert_fusion = bf16[512,16384]{1,0:T(8,128)(2,1)} fusion(bf16[512,16384]{1,0:T(8,128)(2,1)} %copy-done, bf16[256,16384]{1,0:T(8,128)(2,1)} %fusion, bf16[256,16384]{1,0:T(8,128)(2,1)} %slice_bitcast_fusion.1, pred[16384]{0:T(1024)(128)(4,1)S(1)} %add_compare_fusion, bf16[512,512]{0,1:T(8,128)(2,1)S(1)} %collective-permute-done.4, pred[]{:T(512)S(6)} %eq.6, ...), kind=kOutput, calls=%fused_computation | convolution fusion | flops 8658354176 | bytes 51396608 | tf_op jit(solution)/shard_map/dot_general | solution.py:78
  209.6 0.0 reduce-scatter.2.cloned.1.call-update
  209.7 0.1 fusion.8
  209.8 1.0 copy.8
  210.8 3.0 dynamic-slice_bitcast_fusion
  213.9 107.5 %reduce-scatter.2.cloned.1.call-done = bf16[32,16384]{1,0:T(8,128)(2,1)} async-done(((bf16[512,16384]{1,0:T(8,128)(2,1)}), bf16[32,16384]{1,0:T(8,128)(2,1)}) %reduce-scatter.2.cloned.1.call-update) | async-done | bytes 1048592 | tf_op jit(solution)/shard_map/reduce_scatter | solution.py:82
  321.3 2.7 bitcast_convert_fusion
  (13 shorter events, 0.2 us)
Async XLA Ops:
  7.2 163.9 %all-gather.2.cloned.1.call-start = ((), (), s32[]{:S(2)}) async-start(), calls=%async_computation.1 | async-start | bytes 20971520 | tf_op jit(solution)/shard_map/all_gather | solution.py:42
  12.9 308.5 %reduce-scatter.2.cloned.1.call-start = ((), (), s32[]{:S(2)}) async-start(), calls=%async_computation.2 | async-start | bytes 17825792 | tf_op jit(solution)/shard_map/reduce_scatter | solution.py:82
  13.9 39.0 %collective-permute-start = (bf16[2,64,512]{2,1,0:T(8,128)(2,1)S(1)}, bf16[2,64,512]{2,1,0:T(8,128)(2,1)S(1)}, u32[]{:S(2)}, u32[]{:S(2)}) collective-permute-start(bf16[2,64,512]{2,1,0:T(8,128)(2,1)S(1)} %get-tuple-element.6), channel_id=1, source_target_pairs={{0,6},{2,0},{4,2},{6,4},{1,7},{3,1},{5,3},{7,5},{8,14},{10,8},{12,... | collective-permute-start | bytes 393224 | tf_op jit(solution)/shard_map/ppermute | solution.py:8
  18.0 34.5 %collective-permute-start.1 = (bf16[2,64,512]{2,1,0:T(8,128)(2,1)S(1)}, bf16[2,64,512]{2,1,0:T(8,128)(2,1)S(1)}, u32[]{:S(2)}, u32[]{:S(2)}) collective-permute-start(bf16[2,64,512]{2,1,0:T(8,128)(2,1)S(1)} %get-tuple-element.6), channel_id=1, source_target_pairs={{0,2},{2,4},{4,6},{6,0},{1,3},{3,5},{5,7},{7,1},{8,10},{10,12},{12... | collective-permute-start | bytes 393224 | tf_op jit(solution)/shard_map/ppermute | solution.py:8
  33.9 18.3 %copy-start.1 = (bf16[1,2,256,256]{3,2,1,0:T(8,128)(2,1)S(1)}, bf16[1,2,256,256]{3,2,1,0:T(8,128)(2,1)}, u32[]{:S(2)}) copy-start(bf16[1,2,256,256]{3,2,1,0:T(8,128)(2,1)} %param.7) | copy-start | bytes 786436
  46.4 5.9 %copy-start = (bf16[512,16384]{1,0:T(8,128)(2,1)}, bf16[512,16384]{1,0:T(8,128)(2,1)S(1)}, u32[]{:S(2)}) copy-start(bf16[512,16384]{1,0:T(8,128)(2,1)S(1)} %bitcast_multiply_fusion) | copy-start | bytes 50331652
  52.6 7.2 %collective-permute-start.2 = (bf16[2,32,512]{2,1,0:T(8,128)(2,1)S(1)}, bf16[2,32,512]{2,1,0:T(8,128)(2,1)S(1)}, u32[]{:S(2)}, u32[]{:S(2)}) collective-permute-start(bf16[2,32,512]{2,1,0:T(8,128)(2,1)S(1)} %slice.58), channel_id=1, source_target_pairs={{0,2},{2,4},{4,6},{6,0},{1,3},{3,5},{5,7},{7,1},{8,10},{10,12},{12... | collective-permute-start | bytes 196616 | tf_op jit(solution)/shard_map/ppermute | solution.py:8
  52.9 6.9 %collective-permute-start.3 = (bf16[2,32,512]{2,1,0:T(8,128)(2,1)S(1)}, bf16[2,32,512]{2,1,0:T(8,128)(2,1)S(1)}, u32[]{:S(2)}, u32[]{:S(2)}) collective-permute-start(bf16[2,32,512]{2,1,0:T(8,128)(2,1)S(1)} %slice.59), channel_id=1, source_target_pairs={{0,6},{2,0},{4,2},{6,4},{1,7},{3,1},{5,3},{7,5},{8,14},{10,8},{12,... | collective-permute-start | bytes 196616 | tf_op jit(solution)/shard_map/ppermute | solution.py:8
  61.0 117.5 %collective-permute-start.5 = (bf16[256,256]{1,0:T(8,128)(2,1)S(1)}, bf16[256,256]{1,0:T(8,128)(2,1)S(1)}, u32[]{:S(2)}, u32[]{:S(2)}) collective-permute-start(bf16[256,256]{1,0:T(8,128)(2,1)S(1)} %convolution_convert_fusion.2), channel_id=1, source_target_pairs={{0,1},{2,3},{4,5},{6,7},{8,9},{10,11},{12,13},{14,15},{16,17},{18,... | collective-permute-start | bytes 393224 | tf_op jit(solution)/shard_map/ppermute | solution.py:65
  63.8 123.9 %collective-permute-start.4 = (bf16[512,512]{0,1:T(8,128)(2,1)S(1)}, bf16[512,512]{0,1:T(8,128)(2,1)S(1)}, u32[]{:S(2)}, u32[]{:S(2)}) collective-permute-start(bf16[512,512]{0,1:T(8,128)(2,1)S(1)} %pad_maximum_fusion), channel_id=1, source_target_pairs={{0,1},{2,3},{4,5},{6,7},{8,9},{10,11},{12,13},{14,15},{16,17},{18,... | collective-permute-start | bytes 1572872 | tf_op jit(solution)/shard_map/ppermute | solution.py:65
Sparse Core Ops, SparseCore 0:
  13.0 158.0 all-gather.1
  209.8 111.4 reduce-scatter.1

commit v3 on v2

--- a/solution.py
+++ b/solution.py
@@ -66,17 +66,21 @@
     on_root = pcol == 0
     lower_panel = jnp.where(on_root, lower_panel, sent[0])
     lower_pivot = jnp.where(on_root, lower_pivot, sent[1])
-    upper_first = gathered[0]
-    upper_second = (
-        gathered[1].astype(jnp.float32)
-        - jnp.dot(lower_pivot, upper_first, preferred_element_type=jnp.float32)
+    own_pivot = lax.dynamic_slice_in_dim(lower_pivot, row_offset, own_rows, 0)
+    upper_own = (
+        pivot_masked[1].astype(jnp.float32)
+        - jnp.dot(own_pivot, gathered[0], preferred_element_type=jnp.float32)
     ).astype(jnp.bfloat16)
-    upper_own = lax.dynamic_slice_in_dim(upper_second, row_offset, own_rows, 0)
-    stacked = jnp.concatenate([upper_first, upper_second], 0)
+    folded = (
+        lower_panel[:, :block_size].astype(jnp.float32)
+        - jnp.dot(lower_panel[:, block_size:], lower_pivot, preferred_element_type=jnp.float32)
+    ).astype(jnp.bfloat16)
+    multipliers = jnp.concatenate([folded, lower_panel[:, block_size:]], 1)
+    stacked = gathered.reshape(2 * block_size, col_count)
     col_index = lax.axis_index("pcol") * col_count + jnp.arange(col_count, dtype=jnp.int32)
     retained = col_index >= panel_width
     schur_rows = masked.astype(jnp.float32) - jnp.dot(
-        lower_panel, stacked, preferred_element_type=jnp.float32
+        multipliers, stacked, preferred_element_type=jnp.float32
     )
     schur_rows = jnp.where(retained[None, :], schur_rows, jnp.zeros_like(schur_rows))
     summed = lax.psum_scatter(

time: 332 us -> 316 us (0.952)
  waiting for transfers between devices: 217 us -> 203 us
    reduce_scatter x1, waiting for transfers between devices: 107 us -> 94.1 us  [on_device(): lax.psum_scatter(schur_rows.astype(jnp.bfloat16), 'layer', scatter_dimens...]
    unnamed x16 -> x18, local copies, waits for them, and re-layouts: 20.4 us -> 28.4 us
    squeeze x2 -> x1, local copies, waits for them, and re-layouts: 7.52 us -> 0.04 us  [on_device(): second_cols = panel[1]]
    dot_general x2 -> x3, matrix products: 31.1 us -> 31.8 us  [the longest x1 23.3 us: on_device(): jnp.dot(multipliers, stacked, preferred_element_type=jnp.float32)]
  transfers between devices with their start and end apart: 8 -> 8, of which waited for: 3 -> 4; matrix products, arithmetic and copies ran while one was open for 16% -> 16% of each run, Pallas kernels for 0% -> 0%
where the time goes in v3:
time: 316 us; the launch traced here: 315 us
  waiting for transfers between devices  203 us (64%)
  matrix products  33.7 us (11%)
  local copies, waits for them, and re-layouts  32.1 us (10%)
  other arithmetic  21.7 us (7%)
  between operations  14.3 us (5%)
  starting transfers between devices  10.4 us (3%)
    all_gather x1, waiting for transfers between devices, on_device(): gathered = lax.all_gather(pivot_masked, 'prow', axis=1, tiled=True)  104 us
    reduce_scatter x1, waiting for transfers between devices, on_device(): lax.psum_scatter(schur_rows.astype(jnp.bfloat16), 'layer', scatter_dimens...  94.1 us
    unnamed x18, local copies, waits for them, and re-layouts  28.4 us
    dot_general x1, matrix products, on_device(): jnp.dot(multipliers, stacked, preferred_element_type=jnp.float32)  23.3 us
    mul x1, other arithmetic, on_device(): front[0]  12.5 us
    dot_general x1, matrix products, on_device(): jnp.dot(own_pivot, gathered[0], preferred_element_type=jnp.float32)  8.25 us
    ppermute x4, starting transfers between devices, ring(): lax.ppermute(value, axis, [(i, (i + step) % size) for i in range(size)])  7.57 us
  transfers between devices with their start and end apart: 8, of which 4 were waited for; matrix products, arithmetic and copies ran while one was open for 16% of the time, Pallas kernels for 0%

profile of v3, /device:TPU:0, one launch (start us, length us, event | category | flops | bytes accessed | tf_op | source)
XLA Modules:
  0.0 315.4 jit_solution(10199854560285963614)
XLA Ops:
  7.2 0.0 all-gather.2.cloned.1.call-start
  7.2 0.7 convert_bitcast_fusion
  7.9 0.1 broadcast_bitcast_fusion
  8.0 0.1 copy.10
  8.1 4.7 %bitcast_multiply_fusion.1 = bf16[2,64,16384]{2,1,0:T(8,128)(2,1)} fusion(bf16[1,2,64,16384]{3,2,1,0:T(8,128)(2,1)} %param.6, bf16[2,16384]{1,0:T(2,128)(2,1)S(1)} %bitcast.55), kind=kLoop, calls=%fused_computation.6 | loop fusion | flops 2097152 | bytes 8454144 | tf_op jit(solution)/shard_map/mul | solution.py:32
  12.7 0.0 all-gather.2.cloned.1.call-update
  12.7 0.0 reduce-scatter.2.cloned.1.call-start
  12.8 0.9 fusion.26
  13.7 4.2 %collective-permute-start = (bf16[2,64,512]{2,1,0:T(8,128)(2,1)S(1)}, bf16[2,64,512]{2,1,0:T(8,128)(2,1)S(1)}, u32[]{:S(2)}, u32[]{:S(2)}) collective-permute-start(bf16[2,64,512]{2,1,0:T(8,128)(2,1)S(1)} %get-tuple-element.6), channel_id=1, source_target_pairs={{0,6},{2,0},{4,2},{6,4},{1,7},{3,1},{5,3},{7,5},{8,14},{10,8},{12,... | collective-permute-start | bytes 393224 | tf_op jit(solution)/shard_map/ppermute | solution.py:8
  17.9 0.0 collective-permute-start.1
  17.9 0.7 convert_bitcast_fusion.1
  18.6 2.7 mul.35
  21.3 12.5 %copy.9 = bf16[64,8,64,256]{3,1,2,0:T(8,128)(2,1)} copy(bf16[64,8,64,256]{3,2,1,0:T(8,128)(2,1)S(1)} %bitcast.48) | data formatting | bytes 33554432
  33.9 0.0 copy-start.1
  33.9 12.5 %bitcast_multiply_fusion = bf16[512,16384]{1,0:T(8,128)(2,1)S(1)} fusion(bf16[512,16384]{1,0:T(8,128)(2,1)} %bitcast.47, bf16[1,512,16384]{2,1,0:T(8,128)(2,1)} %param.5), kind=kLoop, calls=%fused_computation.4 | loop fusion | flops 8388608 | bytes 50331648 | tf_op jit(solution)/shard_map/mul | solution.py:28
  46.3 0.0 copy-start
  46.3 5.8 %copy-done = bf16[512,16384]{1,0:T(8,128)(2,1)} copy-done((bf16[512,16384]{1,0:T(8,128)(2,1)}, bf16[512,16384]{1,0:T(8,128)(2,1)S(1)}, u32[]{:S(2)}) %copy-start) | copy-done | bytes 16777240
  52.2 0.0 copy-done.1
  52.2 0.3 convolution_convert_fusion.1
  52.4 0.0 collective-permute-done.1
  52.5 0.3 collective-permute-start.2
  52.8 0.0 collective-permute-done
  52.8 3.1 collective-permute-start.3
  55.9 3.8 %collective-permute-done.2 = bf16[2,32,512]{2,1,0:T(8,128)(2,1)S(1)} collective-permute-done((bf16[2,32,512]{2,1,0:T(8,128)(2,1)S(1)}, bf16[2,32,512]{2,1,0:T(8,128)(2,1)S(1)}, u32[]{:S(2)}, u32[]{:S(2)}) %collective-permute-start.2) | collective-permute-done | bytes 65568 | tf_op jit(solution)/shard_map/ppermute | solution.py:8
  59.6 0.0 collective-permute-done.3
  59.7 0.9 constant_dynamic-update-slice_fusion.4
  60.7 1.4 convolution_convert_fusion
  62.2 1.3 collective-permute-start.4
  63.5 0.2 convolution_convert_fusion.2
  63.7 1.5 collective-permute-start.5
  65.2 0.8 collective-permute-done.5
  66.0 0.0 collective-permute-done.4
  66.0 0.1 broadcast_select_fusion
  66.2 0.3 subtract_convert_fusion
  66.5 104.5 %all-gather.2.cloned.1.call-done = bf16[2,256,16384]{2,1,0:T(8,128)(2,1)} async-done(((bf16[2,64,16384]{2,1,0:T(8,128)(2,1)}), bf16[2,256,16384]{2,1,0:T(8,128)(2,1)}) %all-gather.2.cloned.1.call-update) | async-done | bytes 16777232 | tf_op jit(solution)/shard_map/all_gather | solution.py:42
  170.9 23.3 %select_convert_fusion = bf16[512,16384]{1,0:T(8,128)(2,1)} fusion(bf16[512,16384]{1,0:T(8,128)(2,1)} %copy-done, bf16[512,16384]{1,0:T(8,128)(2,1)} %bitcast.53, pred[16384]{0:T(1024)(128)(4,1)S(1)} %add_compare_fusion, bf16[512,256]{0,1:T(8,128)(2,1)S(1)} %slice.72, bf16[512,256]{0,1:T(8,128)(2,1)S(1)} %subtract_convert_fusion), kind=kOutput, calls=%fused_computation | convolution fusion | flops 8624537600 | bytes 50872320 | tf_op jit(solution)/shard_map/dot_general | solution.py:82
  194.2 0.0 reduce-scatter.2.cloned.1.call-update
  194.3 3.4 %copy.11 = bf16[16,8,64,256]{3,2,1,0:T(8,128)(2,1)S(1)} copy(bf16[16,8,64,256]{3,1,2,0:T(8,128)(2,1)} %bitcast.50) | data formatting | bytes 8388608
  197.7 0.3 fusion.2
  198.0 4.5 %copy.12 = f32[8,8,64,256]{3,1,2,0:T(8,128)} copy(f32[8,8,64,256]{3,2,1,0:T(8,128)S(1)} %bitcast.51) | data formatting | bytes 8388608
  202.5 1.0 copy.8
  203.5 8.2 %fusion.1 = bf16[1,64,16384]{2,1,0:T(8,128)(2,1)} fusion(f32[64,16384]{1,0:T(8,128)} %bitcast.49, bf16[2,256,16384]{2,1,0:T(8,128)(2,1)} %all-gather.2.cloned.1.call-done, bf16[256,256]{1,0:T(8,128)(2,1)S(1)} %broadcast_select_fusion.1, s32[]{:T(128)S(6)} %select_n.43), kind=kOutput, calls=%fused_computation.3 | convolution fusion | flops 538968064 | bytes 14712836 | tf_op jit(solution)/shard_map/dot_general | solution.py:72
  211.7 94.1 %reduce-scatter.2.cloned.1.call-done = bf16[32,16384]{1,0:T(8,128)(2,1)} async-done(((bf16[512,16384]{1,0:T(8,128)(2,1)}), bf16[32,16384]{1,0:T(8,128)(2,1)}) %reduce-scatter.2.cloned.1.call-update) | async-done | bytes 1048592 | tf_op jit(solution)/shard_map/reduce_scatter | solution.py:86
  305.9 2.7 bitcast_convert_fusion
  (16 shorter events, 0.2 us)
Async XLA Ops:
  7.2 163.8 %all-gather.2.cloned.1.call-start = ((), (), s32[]{:S(2)}) async-start(), calls=%async_computation.1 | async-start | bytes 20971520 | tf_op jit(solution)/shard_map/all_gather | solution.py:42
  12.7 293.1 %reduce-scatter.2.cloned.1.call-start = ((), (), s32[]{:S(2)}) async-start(), calls=%async_computation.2 | async-start | bytes 17825792 | tf_op jit(solution)/shard_map/reduce_scatter | solution.py:86
  13.7 39.1 %collective-permute-start = (bf16[2,64,512]{2,1,0:T(8,128)(2,1)S(1)}, bf16[2,64,512]{2,1,0:T(8,128)(2,1)S(1)}, u32[]{:S(2)}, u32[]{:S(2)}) collective-permute-start(bf16[2,64,512]{2,1,0:T(8,128)(2,1)S(1)} %get-tuple-element.6), channel_id=1, source_target_pairs={{0,6},{2,0},{4,2},{6,4},{1,7},{3,1},{5,3},{7,5},{8,14},{10,8},{12,... | collective-permute-start | bytes 393224 | tf_op jit(solution)/shard_map/ppermute | solution.py:8
  17.9 34.5 %collective-permute-start.1 = (bf16[2,64,512]{2,1,0:T(8,128)(2,1)S(1)}, bf16[2,64,512]{2,1,0:T(8,128)(2,1)S(1)}, u32[]{:S(2)}, u32[]{:S(2)}) collective-permute-start(bf16[2,64,512]{2,1,0:T(8,128)(2,1)S(1)} %get-tuple-element.6), channel_id=1, source_target_pairs={{0,2},{2,4},{4,6},{6,0},{1,3},{3,5},{5,7},{7,1},{8,10},{10,12},{12... | collective-permute-start | bytes 393224 | tf_op jit(solution)/shard_map/ppermute | solution.py:8
  33.9 18.3 %copy-start.1 = (bf16[1,2,256,256]{3,2,1,0:T(8,128)(2,1)S(1)}, bf16[1,2,256,256]{3,2,1,0:T(8,128)(2,1)}, u32[]{:S(2)}) copy-start(bf16[1,2,256,256]{3,2,1,0:T(8,128)(2,1)} %param.7) | copy-start | bytes 786436
  46.3 5.9 %copy-start = (bf16[512,16384]{1,0:T(8,128)(2,1)}, bf16[512,16384]{1,0:T(8,128)(2,1)S(1)}, u32[]{:S(2)}) copy-start(bf16[512,16384]{1,0:T(8,128)(2,1)S(1)} %bitcast_multiply_fusion) | copy-start | bytes 50331652
  52.5 7.2 %collective-permute-start.2 = (bf16[2,32,512]{2,1,0:T(8,128)(2,1)S(1)}, bf16[2,32,512]{2,1,0:T(8,128)(2,1)S(1)}, u32[]{:S(2)}, u32[]{:S(2)}) collective-permute-start(bf16[2,32,512]{2,1,0:T(8,128)(2,1)S(1)} %slice.68), channel_id=1, source_target_pairs={{0,2},{2,4},{4,6},{6,0},{1,3},{3,5},{5,7},{7,1},{8,10},{10,12},{12... | collective-permute-start | bytes 196616 | tf_op jit(solution)/shard_map/ppermute | solution.py:8
  52.8 6.9 %collective-permute-start.3 = (bf16[2,32,512]{2,1,0:T(8,128)(2,1)S(1)}, bf16[2,32,512]{2,1,0:T(8,128)(2,1)S(1)}, u32[]{:S(2)}, u32[]{:S(2)}) collective-permute-start(bf16[2,32,512]{2,1,0:T(8,128)(2,1)S(1)} %slice.69), channel_id=1, source_target_pairs={{0,6},{2,0},{4,2},{6,4},{1,7},{3,1},{5,3},{7,5},{8,14},{10,8},{12,... | collective-permute-start | bytes 196616 | tf_op jit(solution)/shard_map/ppermute | solution.py:8
  62.2 3.8 %collective-permute-start.4 = (bf16[512,512]{0,1:T(8,128)(2,1)S(1)}, bf16[512,512]{0,1:T(8,128)(2,1)S(1)}, u32[]{:S(2)}, u32[]{:S(2)}) collective-permute-start(bf16[512,512]{0,1:T(8,128)(2,1)S(1)} %pad_maximum_fusion), channel_id=1, source_target_pairs={{0,1},{2,3},{4,5},{6,7},{8,9},{10,11},{12,13},{14,15},{16,17},{18,... | collective-permute-start | bytes 1572872 | tf_op jit(solution)/shard_map/ppermute | solution.py:65
  63.7 2.3 collective-permute-start.5
Sparse Core Ops, SparseCore 0:
  12.9 158.0 all-gather.1
  194.4 111.4 reduce-scatter.1

commit v4 on v3

--- a/solution.py
+++ b/solution.py
@@ -83,9 +83,17 @@
         multipliers, stacked, preferred_element_type=jnp.float32
     )
     schur_rows = jnp.where(retained[None, :], schur_rows, jnp.zeros_like(schur_rows))
+    side = 4
+    by_y = [[x + side * y for y in range(side)] for x in range(side)]
+    by_x = [[x + side * y for x in range(side)] for y in range(side)]
+    partial = lax.psum_scatter(
+        schur_rows.astype(jnp.bfloat16), "layer", scatter_dimension=0, tiled=True,
+        axis_index_groups=by_y,
+    )
     summed = lax.psum_scatter(
-        schur_rows.astype(jnp.bfloat16), "layer", scatter_dimension=0, tiled=True
-    ).astype(jnp.float32)
+        partial.astype(jnp.float32), "layer", scatter_dimension=0, tiled=True,
+        axis_index_groups=by_x,
+    )
     ancestor = summed.reshape(1, 1, summed.shape[0], col_count)
     return (ancestor, lower_panel[None], upper_own[None])
 

time: 316 us -> 438 us (1.39)
  waiting for transfers between devices: 203 us -> 322 us
    reduce_scatter x0 -> x1, waiting for transfers between devices: none -> 63.7 us  [on_device(): lax.psum_scatter(partial.astype(jnp.float32), 'layer', scatter_dimension=...]
    reduce_scatter x1, waiting for transfers between devices: 94.1 us -> 149 us  [on_device(): lax.psum_scatter(schur_rows.astype(jnp.bfloat16), 'layer', scatter_dimens...]
    convert_element_type x0 -> x1, other arithmetic: none -> 6.26 us  [on_device(): partial.astype(jnp.float32)]
    unnamed x18 -> x20, local copies, waits for them, and re-layouts: 28.4 us -> 28.2 us
  transfers between devices with their start and end apart: 8 -> 9, of which waited for: 4 -> 5; matrix products, arithmetic and copies ran while one was open for 16% -> 11% of each run, Pallas kernels for 0% -> 0%
where the time goes in v4:
time: 438 us; the launch traced here: 437 us
  waiting for transfers between devices  322 us (74%)
  matrix products  33 us (8%)
  local copies, waits for them, and re-layouts  32 us (7%)
  other arithmetic  24.9 us (6%)
  between operations  14 us (3%)
  starting transfers between devices  10.5 us (2%)
    reduce_scatter x1, waiting for transfers between devices, on_device(): lax.psum_scatter(schur_rows.astype(jnp.bfloat16), 'layer', scatter_dimens...  149 us
    all_gather x1, waiting for transfers between devices, on_device(): gathered = lax.all_gather(pivot_masked, 'prow', axis=1, tiled=True)  105 us
    reduce_scatter x1, waiting for transfers between devices, on_device(): lax.psum_scatter(partial.astype(jnp.float32), 'layer', scatter_dimension=...  63.7 us
    unnamed x20, local copies, waits for them, and re-layouts  28.2 us
    dot_general x1, matrix products, on_device(): jnp.dot(multipliers, stacked, preferred_element_type=jnp.float32)  23.3 us
    mul x1, other arithmetic, on_device(): front[0]  12.6 us
  transfers between devices with their start and end apart: 9, of which 5 were waited for; matrix products, arithmetic and copies ran while one was open for 11% of the time, Pallas kernels for 0%

profile of v4, /device:TPU:0, one launch (start us, length us, event | category | flops | bytes accessed | tf_op | source)
XLA Modules:
  0.0 436.6 jit_solution(3018374988247187877)
XLA Ops:
  7.2 0.0 copy-start.2
  7.2 0.0 all-gather.2.cloned.1.call-start
  7.2 0.7 convert_bitcast_fusion
  7.9 0.1 broadcast_bitcast_fusion
  8.0 0.1 copy.10
  8.1 4.8 %bitcast_multiply_fusion.1 = bf16[2,64,16384]{2,1,0:T(8,128)(2,1)} fusion(bf16[1,2,64,16384]{3,2,1,0:T(8,128)(2,1)} %param.6, bf16[2,16384]{1,0:T(2,128)(2,1)S(1)} %bitcast.53), kind=kLoop, calls=%fused_computation.6 | loop fusion | flops 2097152 | bytes 8454144 | tf_op jit(solution)/shard_map/mul | solution.py:32
  12.9 0.0 all-gather.2.cloned.1.call-update
  12.9 0.0 reduce-scatter.3.cloned.1.call-start
  12.9 0.9 fusion.26
  13.9 4.2 collective-permute-start
  18.0 0.0 collective-permute-start.1
  18.0 0.0 copy-done.2
  18.1 2.7 mul.35
  20.8 12.4 %copy.9 = bf16[64,8,64,256]{3,1,2,0:T(8,128)(2,1)} copy(bf16[64,8,64,256]{3,2,1,0:T(8,128)(2,1)S(1)} %bitcast.46) | data formatting | bytes 33554432
  33.3 0.0 copy-start.1
  33.3 12.6 %bitcast_multiply_fusion = bf16[512,16384]{1,0:T(8,128)(2,1)S(1)} fusion(bf16[512,16384]{1,0:T(8,128)(2,1)} %bitcast.45, bf16[1,512,16384]{2,1,0:T(8,128)(2,1)} %param.5), kind=kLoop, calls=%fused_computation.4 | loop fusion | flops 8388608 | bytes 50331648 | tf_op jit(solution)/shard_map/mul | solution.py:28
  45.9 0.0 copy-start
  45.9 5.9 %copy-done = bf16[512,16384]{1,0:T(8,128)(2,1)} copy-done((bf16[512,16384]{1,0:T(8,128)(2,1)}, bf16[512,16384]{1,0:T(8,128)(2,1)S(1)}, u32[]{:S(2)}) %copy-start) | copy-done | bytes 16777240
  51.7 0.0 copy-done.1
  51.7 0.3 convolution_convert_fusion.1
  52.0 0.0 collective-permute-done.1
  52.0 0.2 collective-permute-start.2
  52.3 0.0 collective-permute-done
  52.3 3.1 collective-permute-start.3
  55.4 3.8 collective-permute-done.2
  59.2 0.0 collective-permute-done.3
  59.3 0.9 constant_dynamic-update-slice_fusion.4
  60.3 1.4 convolution_convert_fusion
  61.8 1.3 collective-permute-start.4
  63.1 0.2 convolution_convert_fusion.2
  63.3 1.3 collective-permute-start.5
  64.6 0.9 collective-permute-done.5
  65.6 0.0 collective-permute-done.4
  65.6 0.1 broadcast_select_fusion
  65.8 0.3 subtract_convert_fusion
  66.0 105.0 %all-gather.2.cloned.1.call-done = bf16[2,256,16384]{2,1,0:T(8,128)(2,1)} async-done(((bf16[2,64,16384]{2,1,0:T(8,128)(2,1)}), bf16[2,256,16384]{2,1,0:T(8,128)(2,1)}) %all-gather.2.cloned.1.call-update) | async-done | bytes 16777232 | tf_op jit(solution)/shard_map/all_gather | solution.py:42
  171.1 23.3 %select_convert_fusion = bf16[512,16384]{1,0:T(8,128)(2,1)} fusion(bf16[512,16384]{1,0:T(8,128)(2,1)} %copy-done, bf16[512,16384]{1,0:T(8,128)(2,1)} %bitcast.51, pred[16384]{0:T(1024)(128)(4,1)S(1)} %add_compare_fusion, bf16[512,256]{0,1:T(8,128)(2,1)S(1)} %slice.72, bf16[512,256]{0,1:T(8,128)(2,1)S(1)} %subtract_convert_fusion), kind=kOutput, calls=%fused_computation | convolution fusion | flops 8624537600 | bytes 50872320 | tf_op jit(solution)/shard_map/dot_general | solution.py:82
  194.4 0.0 reduce-scatter.3.cloned.1.call-update
  194.4 0.2 reduce-scatter.5.cloned.1.call-start
  194.6 148.8 %reduce-scatter.3.cloned.1.call-done = bf16[128,16384]{1,0:T(8,128)(2,1)} async-done(((bf16[512,16384]{1,0:T(8,128)(2,1)}), bf16[128,16384]{1,0:T(8,128)(2,1)}) %reduce-scatter.3.cloned.1.call-update) | async-done | bytes 4194320 | tf_op jit(solution)/shard_map/reduce_scatter | solution.py:89
  343.4 6.3 %convert_element_type.72 = f32[128,16384]{1,0:T(8,128)} convert(bf16[128,16384]{1,0:T(8,128)(2,1)} %reduce-scatter.3.cloned.1.call-done) | non-fusion elementwise | flops 2097152 | bytes 12582912 | tf_op jit(solution)/shard_map/convert_element_type | solution.py:94
  349.7 0.0 reduce-scatter.5.cloned.1.call-update
  349.7 3.4 copy.11
  353.1 0.3 fusion.2
  353.5 4.3 copy.12
  357.8 1.0 copy.8
  358.8 7.5 %fusion.1 = bf16[1,64,16384]{2,1,0:T(8,128)(2,1)} fusion(f32[64,16384]{1,0:T(8,128)} %bitcast.47, bf16[2,256,16384]{2,1,0:T(8,128)(2,1)} %all-gather.2.cloned.1.call-done, bf16[256,256]{1,0:T(8,128)(2,1)S(1)} %broadcast_select_fusion.1, s32[]{:T(128)S(6)} %select_n.43), kind=kOutput, calls=%fused_computation.3 | convolution fusion | flops 538968064 | bytes 14712836 | tf_op jit(solution)/shard_map/dot_general | solution.py:72
  366.4 63.7 %reduce-scatter.5.cloned.1.call-done = f32[32,16384]{1,0:T(8,128)} async-done(((f32[128,16384]{1,0:T(8,128)}), f32[32,16384]{1,0:T(8,128)}) %reduce-scatter.5.cloned.1.call-update) | async-done | bytes 2097168 | tf_op jit(solution)/shard_map/reduce_scatter | solution.py:93
  (17 shorter events, 0.2 us)
Async XLA Ops:
  7.2 10.9 %copy-start.2 = (s32[1,2,64]{2,1,0:T(2,128)S(1)}, s32[1,2,64]{2,1,0:T(2,128)}, u32[]{:S(2)}) copy-start(s32[1,2,64]{2,1,0:T(2,128)} %param.8) | copy-start | bytes 1540
  7.2 163.9 %all-gather.2.cloned.1.call-start = ((), (), s32[]{:S(2)}) async-start(), calls=%async_computation.2 | async-start | bytes 20971520 | tf_op jit(solution)/shard_map/all_gather | solution.py:42
  12.9 330.6 %reduce-scatter.3.cloned.1.call-start = ((), (), s32[]{:S(2)}) async-start(), calls=%async_computation.3 | async-start | bytes 20971520 | tf_op jit(solution)/shard_map/reduce_scatter | solution.py:89
  13.9 38.4 %collective-permute-start = (bf16[2,64,512]{2,1,0:T(8,128)(2,1)S(1)}, bf16[2,64,512]{2,1,0:T(8,128)(2,1)S(1)}, u32[]{:S(2)}, u32[]{:S(2)}) collective-permute-start(bf16[2,64,512]{2,1,0:T(8,128)(2,1)S(1)} %get-tuple-element.6), channel_id=1, source_target_pairs={{0,6},{2,0},{4,2},{6,4},{1,7},{3,1},{5,3},{7,5},{8,14},{10,8},{12,... | collective-permute-start | bytes 393224 | tf_op jit(solution)/shard_map/ppermute | solution.py:8
  18.0 34.0 %collective-permute-start.1 = (bf16[2,64,512]{2,1,0:T(8,128)(2,1)S(1)}, bf16[2,64,512]{2,1,0:T(8,128)(2,1)S(1)}, u32[]{:S(2)}, u32[]{:S(2)}) collective-permute-start(bf16[2,64,512]{2,1,0:T(8,128)(2,1)S(1)} %get-tuple-element.6), channel_id=1, source_target_pairs={{0,2},{2,4},{4,6},{6,0},{1,3},{3,5},{5,7},{7,1},{8,10},{10,12},{12... | collective-permute-start | bytes 393224 | tf_op jit(solution)/shard_map/ppermute | solution.py:8
  33.3 18.5 %copy-start.1 = (bf16[1,2,256,256]{3,2,1,0:T(8,128)(2,1)S(1)}, bf16[1,2,256,256]{3,2,1,0:T(8,128)(2,1)}, u32[]{:S(2)}) copy-start(bf16[1,2,256,256]{3,2,1,0:T(8,128)(2,1)} %param.7) | copy-start | bytes 786436
  45.9 5.9 %copy-start = (bf16[512,16384]{1,0:T(8,128)(2,1)}, bf16[512,16384]{1,0:T(8,128)(2,1)S(1)}, u32[]{:S(2)}) copy-start(bf16[512,16384]{1,0:T(8,128)(2,1)S(1)} %bitcast_multiply_fusion) | copy-start | bytes 50331652
  52.0 7.2 %collective-permute-start.2 = (bf16[2,32,512]{2,1,0:T(8,128)(2,1)S(1)}, bf16[2,32,512]{2,1,0:T(8,128)(2,1)S(1)}, u32[]{:S(2)}, u32[]{:S(2)}) collective-permute-start(bf16[2,32,512]{2,1,0:T(8,128)(2,1)S(1)} %slice.68), channel_id=1, source_target_pairs={{0,2},{2,4},{4,6},{6,0},{1,3},{3,5},{5,7},{7,1},{8,10},{10,12},{12... | collective-permute-start | bytes 196616 | tf_op jit(solution)/shard_map/ppermute | solution.py:8
  52.3 6.9 %collective-permute-start.3 = (bf16[2,32,512]{2,1,0:T(8,128)(2,1)S(1)}, bf16[2,32,512]{2,1,0:T(8,128)(2,1)S(1)}, u32[]{:S(2)}, u32[]{:S(2)}) collective-permute-start(bf16[2,32,512]{2,1,0:T(8,128)(2,1)S(1)} %slice.69), channel_id=1, source_target_pairs={{0,6},{2,0},{4,2},{6,4},{1,7},{3,1},{5,3},{7,5},{8,14},{10,8},{12,... | collective-permute-start | bytes 196616 | tf_op jit(solution)/shard_map/ppermute | solution.py:8
  61.8 3.8 collective-permute-start.4
  63.3 2.3 collective-permute-start.5
  194.4 235.7 %reduce-scatter.5.cloned.1.call-start = ((), (), s32[]{:S(2)}) async-start(), calls=%async_computation.4 | async-start | bytes 10485760 | tf_op jit(solution)/shard_map/reduce_scatter | solution.py:93
Sparse Core Ops, SparseCore 0:
  13.0 158.0 all-gather.1
  194.5 148.8 reduce-scatter.2
  349.8 80.1 reduce-scatter.4
